TPU v7x, 32 devices: a whole 2x2x4 slice. The times are simulated.
32 devices in a mesh: rep: 4 (over y, core), fsdp: 4 (over z), seq: 2 (over x).
Axes of the slice: x: 2, y: 2, z: 4, core: 2. Of those that a mesh axis runs over, the one named last changes fastest.
Arguments:
- tokens: bfloat16 [16, 1024, 1024], P(('rep', 'fsdp'), 'seq'), may hold values from -6 to 6
- positions: int32 [3, 16, 1024], P(None, ('rep', 'fsdp'), 'seq'), may hold values from 0 to 15
- input_gain: bfloat16 [1024], P('fsdp'), may hold values from 0.5 to 1.5
- input_shift: bfloat16 [1024], P('fsdp'), may hold values from -1.5 to 1.5
- joint_weight: bfloat16 [1024, 3072], P('fsdp'), may hold values from -0.1875 to 0.1875
- joint_bias: bfloat16 [3072], P('fsdp'), may hold values from -1.5 to 1.5
- output_weight: bfloat16 [1024, 1024], P('fsdp'), may hold values from -3 to 3
- output_bias: bfloat16 [1024], P('fsdp'), may hold values from -1.5 to 1.5
- middle_gain: bfloat16 [1024], P('fsdp'), may hold values from 0.5 to 1.5
- middle_shift: bfloat16 [1024], P('fsdp'), may hold values from -1.5 to 1.5
- expand_weight: bfloat16 [1024, 4096], P('fsdp'), may hold values from -0.1875 to 0.1875
- expand_bias: bfloat16 [4096], P('fsdp'), may hold values from -2.5 to 2.5
- reduce_weight: bfloat16 [4096, 1024], P('fsdp'), may hold values from -0.09375 to 0.09375
- reduce_bias: bfloat16 [1024], P('fsdp'), may hold values from -1.5 to 1.5
- cotangent: bfloat16 [16, 1024, 1024], P(('rep', 'fsdp'), 'seq'), may hold values from -6 to 6
Outputs:
- block_output: bfloat16 [16, 1024, 1024], P(('rep', 'fsdp'), 'seq')
- input_gradient: float32 [16, 1024, 1024], P(('rep', 'fsdp'), 'seq')
- input_gain_gradient: float32 [1024], P('fsdp')
- input_shift_gradient: float32 [1024], P('fsdp')
- joint_weight_gradient: float32 [1024, 3072], P('fsdp')
- joint_bias_gradient: float32 [3072], P('fsdp')
- output_weight_gradient: float32 [1024, 1024], P('fsdp')
- output_bias_gradient: float32 [1024], P('fsdp')
- middle_gain_gradient: float32 [1024], P('fsdp')
- middle_shift_gradient: float32 [1024], P('fsdp')
- expand_weight_gradient: float32 [1024, 4096], P('fsdp')
- expand_bias_gradient: float32 [4096], P('fsdp')
- reduce_weight_gradient: float32 [4096, 1024], P('fsdp')
- reduce_bias_gradient: float32 [1024], P('fsdp')
All inputs are finite; a program needn't handle non-finite values.
Results may differ from a plain program's by a relative error of at most 0.018.
Values may be sent and summed in bfloat16 or wider, within the bound.
No kernel may reach another device: no remote copies, remote signals or barrier semaphores. Data moves between devices by JAX's collectives and lax.ppermute only.
A program may use at most 192 MiB of HBM per device.

v0:
```python
import jax
import jax.numpy as jnp
from jax import lax
from jax.sharding import PartitionSpec as P

epsilon = 1e-06


def norm_rows(values, gains, shifts):
    average = jnp.mean(values, axis=-1, keepdims=True)
    centred = values - average
    spread = jnp.mean(centred * centred, axis=-1, keepdims=True)
    return centred * lax.rsqrt(spread + epsilon) * gains + shifts


def rotary_tables(positions):
    counter = jnp.arange(10).astype(jnp.float32)
    frequency = jnp.power(10000.0, -counter / 10.0)
    angles = positions.astype(jnp.float32)[:, :, None] * frequency
    angles = jnp.transpose(angles, (1, 0, 2))
    return (jnp.cos(angles), jnp.sin(angles))


def rotate(values, cosine_part, sine_part):
    length = values.shape[0]
    heads_count = values.shape[1]
    turned = values[:, :, :60].reshape(length, heads_count, 3, 2, 10)
    former = turned[:, :, :, 0, :]
    latter = turned[:, :, :, 1, :]
    cosine_wide = cosine_part[:, None, :, :]
    sine_wide = sine_part[:, None, :, :]
    new_former = former * cosine_wide - latter * sine_wide
    new_latter = latter * cosine_wide + former * sine_wide
    joined = jnp.stack([new_former, new_latter], axis=3).reshape(length, heads_count, 60)
    return jnp.concatenate([joined, values[:, :, 60:]], axis=2)


def exact_gelu(values):
    return jax.nn.gelu(values, approximate=False)


def split_heads(block):
    return block.reshape(block.shape[0], block.shape[1] // 64, 64)


def group_scores(query_heads, key_heads):
    return (
        jnp.einsum("thd,shd->hts", query_heads, key_heads, preferred_element_type=jnp.float32)
        * 0.125
    )


def attend(inputs):
    query_block, key_block, value_block = inputs
    query_heads = split_heads(query_block)
    key_heads = split_heads(key_block)
    value_heads = split_heads(value_block)
    scores = group_scores(query_heads, key_heads)
    row_max = jnp.max(scores, axis=2, keepdims=True)
    raised = jnp.exp(scores - row_max)
    row_total = jnp.sum(raised, axis=2, keepdims=True)
    probs_low = (raised / row_total).astype(jnp.bfloat16)
    mixed = jnp.einsum("hts,shd->thd", probs_low, value_heads, preferred_element_type=jnp.float32)
    return (mixed.reshape(query_block.shape[0], -1), row_max, row_total)


def attend_back(inputs):
    query_block, key_block, value_block, grad_block, row_max, row_total = inputs
    query_heads = split_heads(query_block)
    key_heads = split_heads(key_block)
    value_heads = split_heads(value_block)
    grad_heads = split_heads(grad_block)
    scores = group_scores(query_heads, key_heads)
    probs = jnp.exp(scores - row_max) / row_total
    probs_low = probs.astype(jnp.bfloat16)
    grad_probs = jnp.einsum(
        "thd,shd->hts", grad_heads, value_heads, preferred_element_type=jnp.float32
    )
    value_grad = jnp.einsum(
        "hts,thd->shd", probs_low, grad_heads, preferred_element_type=jnp.float32
    )
    inner = jnp.sum(grad_probs * probs, axis=2, keepdims=True)
    grad_scores = (probs * (grad_probs - inner)).astype(jnp.bfloat16)
    query_grad = (
        jnp.einsum("hts,shd->thd", grad_scores, key_heads, preferred_element_type=jnp.float32)
        * 0.125
    )
    key_grad = (
        jnp.einsum("hts,thd->shd", grad_scores, query_heads, preferred_element_type=jnp.float32)
        * 0.125
    )
    return (
        query_grad.reshape(query_block.shape[0], -1),
        key_grad.reshape(key_block.shape[0], -1),
        value_grad.reshape(key_block.shape[0], -1),
    )


def local(
    tokens,
    positions,
    input_gain,
    input_shift,
    joint_weight,
    joint_bias,
    output_weight,
    output_bias,
    middle_gain,
    middle_shift,
    expand_weight,
    expand_bias,
    reduce_weight,
    reduce_bias,
    cotangent,
):
    shards = (
        input_gain,
        input_shift,
        joint_weight,
        joint_bias,
        output_weight,
        output_bias,
        middle_gain,
        middle_shift,
        expand_weight,
        expand_bias,
        reduce_weight,
        reduce_bias,
    )
    gathered = (
        lax.all_gather(shards[0], "fsdp", axis=0, tiled=True),
        lax.all_gather(shards[1], "fsdp", axis=0, tiled=True),
        lax.all_gather(shards[2], "fsdp", axis=0, tiled=True),
        lax.all_gather(shards[3], "fsdp", axis=0, tiled=True),
        lax.all_gather(shards[4], "fsdp", axis=0, tiled=True),
        lax.all_gather(shards[5], "fsdp", axis=0, tiled=True),
        lax.all_gather(shards[6], "fsdp", axis=0, tiled=True),
        lax.all_gather(shards[7], "fsdp", axis=0, tiled=True),
        lax.all_gather(shards[8], "fsdp", axis=0, tiled=True),
        lax.all_gather(shards[9], "fsdp", axis=0, tiled=True),
        lax.all_gather(shards[10], "fsdp", axis=0, tiled=True),
        lax.all_gather(shards[11], "fsdp", axis=0, tiled=True),
    )
    row_count = tokens.shape[1]
    width = tokens.shape[2]
    head_count = width // 64
    per_group = min(4, head_count)
    group_count = head_count // per_group
    group_width = per_group * 64

    def to_groups(block):
        return jnp.transpose(block.reshape(block.shape[0], group_count, group_width), (1, 0, 2))

    def from_groups(block):
        return jnp.transpose(block, (1, 0, 2)).reshape(block.shape[1], width)

    residual_in = tokens[0].astype(jnp.float32)
    cosine_part, sine_part = rotary_tables(positions[:, 0, :])
    normed_in = norm_rows(
        residual_in, gathered[0].astype(jnp.float32), gathered[1].astype(jnp.float32)
    ).astype(jnp.bfloat16)
    projected = jnp.dot(normed_in, gathered[2], preferred_element_type=jnp.float32) + gathered[
        3
    ].astype(jnp.float32)
    queries = (
        rotate(projected[:, :width].reshape(row_count, head_count, 64), cosine_part, sine_part)
        .astype(jnp.bfloat16)
        .reshape(row_count, width)
    )
    keys = (
        rotate(
            projected[:, width : 2 * width].reshape(row_count, head_count, 64),
            cosine_part,
            sine_part,
        )
        .astype(jnp.bfloat16)
        .reshape(row_count, width)
    )
    values = projected[:, 2 * width :].astype(jnp.bfloat16)
    query_groups = to_groups(queries)
    key_all, value_all = (
        lax.all_gather(to_groups(keys), "seq", axis=1, tiled=True),
        lax.all_gather(to_groups(values), "seq", axis=1, tiled=True),
    )
    mixed, row_max, row_total = lax.map(attend, (query_groups, key_all, value_all))
    attended = from_groups(mixed).astype(jnp.bfloat16)
    residual_mid = residual_in + (
        jnp.dot(attended, gathered[4], preferred_element_type=jnp.float32)
        + gathered[5].astype(jnp.float32)
    )
    normed_mid = norm_rows(
        residual_mid, gathered[6].astype(jnp.float32), gathered[7].astype(jnp.float32)
    ).astype(jnp.bfloat16)
    upper = jnp.dot(normed_mid, gathered[8], preferred_element_type=jnp.float32) + gathered[
        9
    ].astype(jnp.float32)
    hidden = exact_gelu(upper).astype(jnp.bfloat16)
    result = residual_mid + (
        jnp.dot(hidden, gathered[10], preferred_element_type=jnp.float32)
        + gathered[11].astype(jnp.float32)
    )
    block_output = result.astype(jnp.bfloat16)[None]
    again = (
        lax.all_gather(shards[0], "fsdp", axis=0, tiled=True),
        lax.all_gather(shards[1], "fsdp", axis=0, tiled=True),
        lax.all_gather(shards[2], "fsdp", axis=0, tiled=True),
        lax.all_gather(shards[3], "fsdp", axis=0, tiled=True),
        lax.all_gather(shards[4], "fsdp", axis=0, tiled=True),
        lax.all_gather(shards[5], "fsdp", axis=0, tiled=True),
        lax.all_gather(shards[6], "fsdp", axis=0, tiled=True),
        lax.all_gather(shards[7], "fsdp", axis=0, tiled=True),
        lax.all_gather(shards[8], "fsdp", axis=0, tiled=True),
        lax.all_gather(shards[9], "fsdp", axis=0, tiled=True),
        lax.all_gather(shards[10], "fsdp", axis=0, tiled=True),
        lax.all_gather(shards[11], "fsdp", axis=0, tiled=True),
    )
    grad_low = cotangent[0]
    grad_out = grad_low.astype(jnp.float32)
    reduce_term = jnp.einsum("tf,td->fd", hidden, grad_low, preferred_element_type=jnp.float32)
    reduce_offset_term = jnp.sum(grad_out, axis=0)
    grad_hidden = jnp.einsum("td,fd->tf", grad_low, again[10], preferred_element_type=jnp.float32)
    gelu_pull = jax.vjp(exact_gelu, upper)[1]
    grad_upper = gelu_pull(grad_hidden)[0].astype(jnp.bfloat16)
    expand_term = jnp.einsum(
        "td,tf->df", normed_mid, grad_upper, preferred_element_type=jnp.float32
    )
    expand_offset_term = jnp.sum(grad_upper.astype(jnp.float32), axis=0)
    grad_mid_norm = jnp.einsum(
        "tf,df->td", grad_upper, again[8], preferred_element_type=jnp.float32
    )
    middle_pull = jax.vjp(
        norm_rows, residual_mid, again[6].astype(jnp.float32), again[7].astype(jnp.float32)
    )[1]
    grad_mid_in, middle_gain_term, middle_shift_term = middle_pull(grad_mid_norm)
    grad_resid = grad_out + grad_mid_in
    grad_branch = grad_resid.astype(jnp.bfloat16)
    output_term = jnp.einsum("td,te->de", attended, grad_branch, preferred_element_type=jnp.float32)
    output_offset_term = jnp.sum(grad_branch.astype(jnp.float32), axis=0)
    grad_attended = jnp.einsum(
        "te,de->td", grad_branch, again[4], preferred_element_type=jnp.float32
    ).astype(jnp.bfloat16)
    query_grad, key_grad, value_grad = lax.map(
        attend_back,
        (query_groups, key_all, value_all, to_groups(grad_attended), row_max, row_total),
    )
    key_share, value_share = (
        lax.psum_scatter(
            key_grad.astype(jnp.bfloat16), "seq", scatter_dimension=1, tiled=True
        ).astype(jnp.float32),
        lax.psum_scatter(
            value_grad.astype(jnp.bfloat16), "seq", scatter_dimension=1, tiled=True
        ).astype(jnp.float32),
    )
    grad_query = rotate(
        from_groups(query_grad).reshape(row_count, head_count, 64), cosine_part, -sine_part
    ).reshape(row_count, width)
    grad_key = rotate(
        from_groups(key_share).reshape(row_count, head_count, 64), cosine_part, -sine_part
    ).reshape(row_count, width)
    grad_value = from_groups(value_share)
    grad_projected = jnp.concatenate([grad_query, grad_key, grad_value], axis=1).astype(
        jnp.bfloat16
    )
    joint_term = jnp.einsum(
        "td,te->de", normed_in, grad_projected, preferred_element_type=jnp.float32
    )
    joint_offset_term = jnp.sum(grad_projected.astype(jnp.float32), axis=0)
    grad_in_norm = jnp.einsum(
        "te,de->td", grad_projected, again[2], preferred_element_type=jnp.float32
    )
    input_pull = jax.vjp(
        norm_rows, residual_in, again[0].astype(jnp.float32), again[1].astype(jnp.float32)
    )[1]
    grad_first_in, input_gain_term, input_shift_term = input_pull(grad_in_norm)
    input_gradient = (grad_resid + grad_first_in)[None]
    terms = (
        input_gain_term,
        input_shift_term,
        joint_term,
        joint_offset_term,
        output_term,
        output_offset_term,
        middle_gain_term,
        middle_shift_term,
        expand_term,
        expand_offset_term,
        reduce_term,
        reduce_offset_term,
    )
    owned = (
        lax.psum_scatter(
            terms[0].astype(jnp.bfloat16), "fsdp", scatter_dimension=0, tiled=True
        ).astype(jnp.float32),
        lax.psum_scatter(
            terms[1].astype(jnp.bfloat16), "fsdp", scatter_dimension=0, tiled=True
        ).astype(jnp.float32),
        lax.psum_scatter(
            terms[2].astype(jnp.bfloat16), "fsdp", scatter_dimension=0, tiled=True
        ).astype(jnp.float32),
        lax.psum_scatter(
            terms[3].astype(jnp.bfloat16), "fsdp", scatter_dimension=0, tiled=True
        ).astype(jnp.float32),
        lax.psum_scatter(
            terms[4].astype(jnp.bfloat16), "fsdp", scatter_dimension=0, tiled=True
        ).astype(jnp.float32),
        lax.psum_scatter(
            terms[5].astype(jnp.bfloat16), "fsdp", scatter_dimension=0, tiled=True
        ).astype(jnp.float32),
        lax.psum_scatter(
            terms[6].astype(jnp.bfloat16), "fsdp", scatter_dimension=0, tiled=True
        ).astype(jnp.float32),
        lax.psum_scatter(
            terms[7].astype(jnp.bfloat16), "fsdp", scatter_dimension=0, tiled=True
        ).astype(jnp.float32),
        lax.psum_scatter(
            terms[8].astype(jnp.bfloat16), "fsdp", scatter_dimension=0, tiled=True
        ).astype(jnp.float32),
        lax.psum_scatter(
            terms[9].astype(jnp.bfloat16), "fsdp", scatter_dimension=0, tiled=True
        ).astype(jnp.float32),
        lax.psum_scatter(
            terms[10].astype(jnp.bfloat16), "fsdp", scatter_dimension=0, tiled=True
        ).astype(jnp.float32),
        lax.psum_scatter(
            terms[11].astype(jnp.bfloat16), "fsdp", scatter_dimension=0, tiled=True
        ).astype(jnp.float32),
    )
    summed = (
        lax.psum(owned[0].astype(jnp.bfloat16), ("rep", "seq")).astype(jnp.float32),
        lax.psum(owned[1].astype(jnp.bfloat16), ("rep", "seq")).astype(jnp.float32),
        lax.psum(owned[2].astype(jnp.bfloat16), ("rep", "seq")).astype(jnp.float32),
        lax.psum(owned[3].astype(jnp.bfloat16), ("rep", "seq")).astype(jnp.float32),
        lax.psum(owned[4].astype(jnp.bfloat16), ("rep", "seq")).astype(jnp.float32),
        lax.psum(owned[5].astype(jnp.bfloat16), ("rep", "seq")).astype(jnp.float32),
        lax.psum(owned[6].astype(jnp.bfloat16), ("rep", "seq")).astype(jnp.float32),
        lax.psum(owned[7].astype(jnp.bfloat16), ("rep", "seq")).astype(jnp.float32),
        lax.psum(owned[8].astype(jnp.bfloat16), ("rep", "seq")).astype(jnp.float32),
        lax.psum(owned[9].astype(jnp.bfloat16), ("rep", "seq")).astype(jnp.float32),
        lax.psum(owned[10].astype(jnp.bfloat16), ("rep", "seq")).astype(jnp.float32),
        lax.psum(owned[11].astype(jnp.bfloat16), ("rep", "seq")).astype(jnp.float32),
    )
    return (
        block_output,
        input_gradient,
        summed[0],
        summed[1],
        summed[2],
        summed[3],
        summed[4],
        summed[5],
        summed[6],
        summed[7],
        summed[8],
        summed[9],
        summed[10],
        summed[11],
    )


def solution(mesh):
    return jax.shard_map(
        local,
        mesh=mesh,
        in_specs=(
            P(("rep", "fsdp"), "seq", None),
            P(None, ("rep", "fsdp"), "seq"),
            P("fsdp"),
            P("fsdp"),
            P("fsdp", None),
            P("fsdp"),
            P("fsdp", None),
            P("fsdp"),
            P("fsdp"),
            P("fsdp"),
            P("fsdp", None),
            P("fsdp"),
            P("fsdp", None),
            P("fsdp"),
            P(("rep", "fsdp"), "seq", None),
        ),
        out_specs=(
            P(("rep", "fsdp"), "seq", None),
            P(("rep", "fsdp"), "seq", None),
            P("fsdp"),
            P("fsdp"),
            P("fsdp", None),
            P("fsdp"),
            P("fsdp", None),
            P("fsdp"),
            P("fsdp"),
            P("fsdp"),
            P("fsdp", None),
            P("fsdp"),
            P("fsdp", None),
            P("fsdp"),
        ),
        check_vma=False,
    )
```

profile of v0, /device:TPU:0, one launch (start us, length us, event | category | flops | bytes accessed | tf_op | source)
XLA Modules:
  0.0 1273.0 jit_solution(16139119386478265900)
XLA Ops:
  8.6 14.8 %all-gather.2 = bf16[4,1,768]{2,1,0:T(2,128)(2,1)S(1)} all-gather(bf16[1,1,768]{2,1,0:T(2,128)(2,1)S(1)} %reshape.244), channel_id=1, replica_groups=mesh['rep'=4,'fsdp'=4,'seq'=2] {'fsdp'}, dimensions={0}, use_global_device_ids=true | all-gather | bytes 7680 | tf_op jit(solution)/shard_map/all_gather | solution.py:134
  24.2 12.4 all-gather.1
  37.3 8.0 all-gather
  49.0 78.8 %all-gather.14.cloned.1.call-done = bf16[1024,3072]{1,0:T(8,128)(2,1)} async-done(((bf16[256,3072]{1,0:T(8,128)(2,1)}), bf16[1024,3072]{1,0:T(8,128)(2,1)}) %all-gather.14.cloned.1.call-update) | async-done | bytes 6291472 | tf_op jit(solution)/shard_map/all_gather | solution.py:133
  127.8 6.1 convolution_add_fusion
  159.4 8.0 all-gather.3
  167.4 11.9 all_gather.59
  179.4 8.3 all-gather.5
  187.7 9.1 all-gather.4
  198.8 5.9 all-gather.18.cloned.1.call-done
  204.7 31.5 %while.30 = (s32[]{:T(128)}, bf16[4,512,256]{1,2,0:T(8,128)(2,1)S(1)}, f32[4,4,512,1]{2,1,3,0:T(4,128)S(1)}, f32[4,4,512,1]{2,1,3,0:T(4,128)S(1)}, bf16[4,1024,2...) while((s32[]{:T(128)}, ...), condition=%wide.region_5.6_spmd.clone, body=%wide.region_2.5_spmd.sunk.clone | while | flops 555741184 | bytes 29958248 | solution.py:185
  236.2 15.6 %all-gather.20.cloned.1.call-done = bf16[1024,1024]{1,0:T(8,128)(2,1)} async-done(((bf16[256,1024]{1,0:T(8,128)(2,1)}), bf16[1024,1024]{1,0:T(8,128)(2,1)}) %all-gather.20.cloned.1.call-update) | async-done | bytes 2097168 | tf_op jit(solution)/shard_map/all_gather | solution.py:135
  255.5 146.2 %all-gather.22.cloned.1.call-done = bf16[1024,4096]{1,0:T(8,128)(2,1)} async-done(((bf16[256,4096]{1,0:T(8,128)(2,1)}), bf16[1024,4096]{1,0:T(8,128)(2,1)}) %all-gather.22.cloned.1.call-update) | async-done | bytes 8388624 | tf_op jit(solution)/shard_map/all_gather | solution.py:139
  401.7 27.6 %multiply_convert_fusion.1 = (bf16[512,4096]{1,0:T(8,128)(2,1)}, f32[512,4096]{1,0:T(8,128)}, f32[512,4096]{1,0:T(8,128)}) fusion(f32[4096]{0:T(1024)S(1)} %convert_element_type.220, bf16[1024,4096]{1,0:T(8,128)(2,1)} %all-gather.22.cloned.1.call-done, f32[512,1024]{1,0:T(8,128)S(1)} %get-tuple-element.210, f32[1024]{0:T(1024)S(1)} %bitcast.295, ...), kind=kOutput, calls=%fused_computation.31 | convolution fusion | flops 4436000768 | bytes 31485952 | tf_op jit(solution)/shard_map/dot_general | solution.py:194
  429.3 121.7 %all-gather.24.cloned.1.call-done = bf16[4096,1024]{1,0:T(8,128)(2,1)} async-done(((bf16[1024,1024]{1,0:T(8,128)(2,1)}), bf16[4096,1024]{1,0:T(8,128)(2,1)}) %all-gather.24.cloned.1.call-update) | async-done | bytes 8388624 | tf_op jit(solution)/shard_map/all_gather | solution.py:141
  550.9 15.9 %fusion.47 = (bf16[4096]{0:T(1024)(128)(2,1)}, bf16[512,4096]{1,0:T(8,128)(2,1)}) fusion(f32[512,4096]{1,0:T(8,128)} %get-tuple-element.179, bf16[4096,1024]{1,0:T(8,128)(2,1)} %all-gather.24.cloned.1.call-done, bf16[1,512,1024]{2,1,0:T(8,128)(2,1)S(1)} %copy-done.7, f32[512,4096]{1,0:T(8,128)} %get-tuple-element.211, f32[4096]{0:T(1024)S(1)} %convert_element_type.220), kind=kOutput, calls=%fused_computation.125 | convolution fusion | flops 4328517632 | bytes 30433280 | tf_op jit(solution)/shard_map/td,fd->tf/dot_general | solution.py:221
  566.9 7.6 multiply_reduce_fusion.2
  582.3 47.7 %while.31 = (s32[]{:T(128)}, f32[4,512,256]{1,2,0:T(8,128)S(1)}, bf16[4,1024,256]{1,2,0:T(8,128)(2,1)}, bf16[4,1024,256]{1,2,0:T(8,128)(2,1)}, bf16[4,1024,256]{...) while((s32[]{:T(128)}, f32[4,512,256]{1,2,0:T(8,128)S(1)}, ...), condition=%wide.region_12.13_spmd.clone, body=%wide.region_10.12_spmd.sunk.clone | while | flops 1361704960 | bytes 73465992 | solution.py:242
  639.0 21.3 %reduce-scatter.7.cloned.1.call-done = bf16[4,512,256]{1,2,0:T(8,128)(2,1)} async-done(((bf16[4,1024,256]{1,2,0:T(8,128)(2,1)}), bf16[4,512,256]{1,2,0:T(8,128)(2,1)}) %reduce-scatter.7.cloned.1.call-update) | async-done | bytes 1048592 | tf_op jit(solution)/shard_map/reduce_scatter | solution.py:247
  665.8 28.7 %reduce-scatter.9.cloned.1.call-done = bf16[4,512,256]{1,2,0:T(8,128)(2,1)} async-done(((bf16[4,1024,256]{1,2,0:T(8,128)(2,1)}), bf16[4,512,256]{1,2,0:T(8,128)(2,1)}) %reduce-scatter.9.cloned.1.call-update) | async-done | bytes 1048592 | tf_op jit(solution)/shard_map/reduce_scatter | solution.py:250
  694.5 7.7 convolution_convert_fusion.2
  704.0 9.2 convolution_convert_fusion.1
  713.5 10.4 convolution_convert_fusion
  724.5 11.5 all-gather.6
  740.5 112.2 %reduce-scatter.11.cloned.1.call-done = bf16[256,3072]{1,0:T(8,128)(2,1)} async-done(((bf16[1024,3072]{1,0:T(8,128)(2,1)}), bf16[256,3072]{1,0:T(8,128)(2,1)}) %reduce-scatter.11.cloned.1.call-update) | async-done | bytes 1572880 | tf_op jit(solution)/shard_map/reduce_scatter | solution.py:297
  852.7 147.5 %reduce-scatter.15.cloned.1.call-done = bf16[256,4096]{1,0:T(8,128)(2,1)} async-done(((bf16[1024,4096]{1,0:T(8,128)(2,1)}), bf16[256,4096]{1,0:T(8,128)(2,1)}) %reduce-scatter.15.cloned.1.call-update) | async-done | bytes 2097168 | tf_op jit(solution)/shard_map/reduce_scatter | solution.py:315
  1000.1 147.5 %reduce-scatter.17.cloned.1.call-done = bf16[1024,1024]{1,0:T(8,128)(2,1)} async-done(((bf16[4096,1024]{1,0:T(8,128)(2,1)}), bf16[1024,1024]{1,0:T(8,128)(2,1)}) %reduce-scatter.17.cloned.1.call-update) | async-done | bytes 2097168 | tf_op jit(solution)/shard_map/reduce_scatter | solution.py:321
  1147.7 10.3 fusion.24
  1157.9 6.8 fusion.40
  1167.2 18.9 %all-reduce.10 = (bf16[1024]{0:T(1024)(128)(2,1)S(1)}, bf16[1024]{0:T(1024)(128)(2,1)S(1)}, bf16[3072]{0:T(1024)(128)(2,1)S(1)}, bf16[1024]{0:T(1024)(128)(2,1)S...) all-reduce(bf16[1024]{0:T(1024)(128)(2,1)S(1)} %get-tuple-element.1, ...), channel_id=4, replica_groups=mesh['rep'=4,'fsdp'=4,'seq'=2] {'fsdp'}, use_global_device_ids=true, to_apply=%region_18.19.clone | all-reduce | flops 13312 | bytes 53248
  1186.6 14.8 %all-reduce.8 = (bf16[256]{0:T(256)(128)(2,1)S(1)}, bf16[256]{0:T(256)(128)(2,1)S(1)}, bf16[768]{0:T(1024)(128)(2,1)S(1)}, bf16[256]{0:T(256)(128)(2,1)S(1)}, bf...) all-reduce(bf16[256]{0:T(256)(128)(2,1)S(1)} %dynamic-slice.1, ...), channel_id=1, replica_groups=mesh['rep'=4,'fsdp'=4,'seq'=2] {'rep','seq'}, use_global_device_ids=true, to_apply=%region_19.20 | all-reduce | flops 3328 | bytes 13312 | tf_op jit(solution)/shard_map/psum | solution.py:329
  1210.2 46.2 %all-reduce.13.cloned.1.call-done = (bf16[256,3072]{1,0:T(8,128)(2,1)}, bf16[256,1024]{1,0:T(8,128)(2,1)}, bf16[256,4096]{1,0:T(8,128)(2,1)}, bf16[1024,1024]{1,0:T(8,128)(2,1)}) async-done(((bf16[256,3072]{1,0:T(8,128)(2,1)}, bf16[256,1024]{1,0:T(8,128)(2,1)}, bf16[256,4096]{1,0:T(8,128)(2,1)}, bf16[1024,1024]{1,0:T(8,128)(2,1)}), (bf16[256,3072]{1,0:T(8,128)(2,1)}, bf16[256,1024]{1,0:T(8,128)(2,1)}, ...) | async-done | bytes 6291472 | tf_op jit(solution)/shard_map/psum | solution.py:331
  (324 shorter events, 164.6 us)
Async XLA Ops:
  7.2 120.6 %all-gather.14.cloned.1.call-start = ((), (), s32[]{:S(2)}) async-start(), calls=%async_computation.6 | async-start | bytes 7864320 | tf_op jit(solution)/shard_map/all_gather | solution.py:133
  7.9 190.9 %all-gather.16.cloned.1.call-start = ((), (), s32[]{:S(2)}) async-start(), calls=%async_computation.7 | async-start | bytes 3145728 | tf_op jit(solution)/shard_map/all_gather | solution.py:183
  36.6 91.2 %copy-start.46 = (f32[4,1,256]{2,1,0:T(1,128)}, f32[4,1,256]{2,1,0:T(1,128)S(1)}, u32[]{:S(2)}) copy-start(f32[4,1,256]{2,1,0:T(1,128)S(1)} %convert_element_type.251) | copy-start | bytes 12292
  45.3 82.5 %copy-start.27 = (f32[4,1,256]{2,1,0:T(1,128)}, f32[4,1,256]{2,1,0:T(1,128)S(1)}, u32[]{:S(2)}) copy-start(f32[4,1,256]{2,1,0:T(1,128)S(1)} %convert_element_type.250) | copy-start | bytes 12292
  46.7 81.0 %copy-start.29 = (f32[512]{0:T(512)}, f32[512]{0:T(512)S(1)}, u32[]{:S(2)}) copy-start(f32[512]{0:T(512)S(1)} %broadcast_multiply_fusion.1) | copy-start | bytes 6148
  49.0 78.8 %copy-start.35 = (f32[512]{0:T(512)}, f32[512]{0:T(512)S(1)}, u32[]{:S(2)}) copy-start(f32[512]{0:T(512)S(1)} %fusion.32) | copy-start | bytes 6148
  138.0 66.7 %all-gather.18.cloned.1.call-start = ((), (), s32[]{:S(2)}) async-start(), calls=%async_computation.8 | async-start | bytes 3145728 | tf_op jit(solution)/shard_map/all_gather | solution.py:182
  155.9 31.8 %copy-start.56 = (bf16[256]{0:T(256)(128)(2,1)S(1)}, bf16[256]{0:T(256)(128)(2,1)}, u32[]{:S(2)}) copy-start(bf16[256]{0:T(256)(128)(2,1)} %param.27) | copy-start | bytes 1540
  157.5 94.3 %all-gather.20.cloned.1.call-start = ((), (), s32[]{:S(2)}) async-start(), calls=%async_computation.9 | async-start | bytes 2621440 | tf_op jit(solution)/shard_map/all_gather | solution.py:135
  158.1 243.6 %all-gather.22.cloned.1.call-start = ((), (), s32[]{:S(2)}) async-start(), calls=%async_computation.10 | async-start | bytes 10485760 | tf_op jit(solution)/shard_map/all_gather | solution.py:139
  158.7 392.3 %all-gather.24.cloned.1.call-start = ((), (), s32[]{:S(2)}) async-start(), calls=%async_computation.11 | async-start | bytes 10485760 | tf_op jit(solution)/shard_map/all_gather | solution.py:141
  159.3 501.0 %reduce-scatter.7.cloned.1.call-start = ((), (), s32[]{:S(2)}) async-start(), calls=%async_computation.12 | async-start | bytes 3145728 | tf_op jit(solution)/shard_map/reduce_scatter | solution.py:247
  187.7 214.0 %copy-start.48 = (f32[4,1,256]{2,1,0:T(1,128)}, f32[4,1,256]{2,1,0:T(1,128)S(1)}, u32[]{:S(2)}) copy-start(f32[4,1,256]{2,1,0:T(1,128)S(1)} %convert_element_type.255) | copy-start | bytes 12292
  196.8 377.6 %copy-start.39 = (f32[4,1,256]{2,1,0:T(1,128)}, f32[4,1,256]{2,1,0:T(1,128)S(1)}, u32[]{:S(2)}) copy-start(f32[4,1,256]{2,1,0:T(1,128)S(1)} %convert_element_type.254) | copy-start | bytes 12292
  204.7 47.1 %copy-start = (bf16[1,512,1024]{2,1,0:T(8,128)(2,1)S(1)}, bf16[1,512,1024]{2,1,0:T(8,128)(2,1)}, u32[]{:S(2)}) copy-start(bf16[1,512,1024]{2,1,0:T(8,128)(2,1)} %param.19) | copy-start | bytes 3145732
  255.1 319.3 %copy-start.4 = (f32[512,1024]{1,0:T(8,128)}, f32[512,1024]{1,0:T(8,128)S(1)}, u32[]{:S(2)}) copy-start(f32[512,1024]{1,0:T(8,128)S(1)} %get-tuple-element.210) | copy-start | bytes 6291460
  255.1 319.3 %copy-start.37 = (f32[512]{0:T(512)}, f32[512]{0:T(512)S(1)}, u32[]{:S(2)}) copy-start(f32[512]{0:T(512)S(1)} %broadcast_multiply_fusion) | copy-start | bytes 6148
  255.5 319.0 %copy-start.42 = (f32[512]{0:T(512)}, f32[512]{0:T(512)S(1)}, u32[]{:S(2)}) copy-start(f32[512]{0:T(512)S(1)} %fusion.33) | copy-start | bytes 6148
  401.7 149.3 %copy-start.7 = (bf16[1,512,1024]{2,1,0:T(8,128)(2,1)S(1)}, bf16[1,512,1024]{2,1,0:T(8,128)(2,1)}, u32[]{:S(2)}) copy-start(bf16[1,512,1024]{2,1,0:T(8,128)(2,1)} %param.33) | copy-start | bytes 3145732
  630.1 64.4 %reduce-scatter.9.cloned.1.call-start = ((), (), s32[]{:S(2)}) async-start(), calls=%async_computation.13 | async-start | bytes 3145728 | tf_op jit(solution)/shard_map/reduce_scatter | solution.py:250
  630.8 109.7 %reduce-scatter.13.cloned.1.call-start = ((), (), s32[]{:S(2)}) async-start(), calls=%async_computation.15 | async-start | bytes 2621440 | tf_op jit(solution)/shard_map/reduce_scatter | solution.py:303
  635.9 216.8 %reduce-scatter.11.cloned.1.call-start = ((), (), s32[]{:S(2)}) async-start(), calls=%async_computation.14 | async-start | bytes 7864320 | tf_op jit(solution)/shard_map/reduce_scatter | solution.py:297
  664.3 30.2 %copy-start.1 = (bf16[1,512,1024]{2,1,0:T(8,128)(2,1)S(1)}, bf16[1,512,1024]{2,1,0:T(8,128)(2,1)}, u32[]{:S(2)}) copy-start(bf16[1,512,1024]{2,1,0:T(8,128)(2,1)} %param.19) | copy-start | bytes 3145732
  664.3 30.1 %copy-start.28 = (f32[4,1,256]{2,1,0:T(1,128)S(1)}, f32[4,1,256]{2,1,0:T(1,128)}, u32[]{:S(2)}) copy-start(f32[4,1,256]{2,1,0:T(1,128)} %copy-done.27) | copy-start | bytes 12292
  664.3 30.1 %copy-start.30 = (f32[512]{0:T(512)S(1)}, f32[512]{0:T(512)}, u32[]{:S(2)}) copy-start(f32[512]{0:T(512)} %copy-done.29) | copy-start | bytes 6148
  664.3 30.1 %copy-start.36 = (f32[512]{0:T(512)S(1)}, f32[512]{0:T(512)}, u32[]{:S(2)}) copy-start(f32[512]{0:T(512)} %copy-done.35) | copy-start | bytes 6148
  664.4 30.1 %copy-start.47 = (f32[4,1,256]{2,1,0:T(1,128)S(1)}, f32[4,1,256]{2,1,0:T(1,128)}, u32[]{:S(2)}) copy-start(f32[4,1,256]{2,1,0:T(1,128)} %copy-done.46) | copy-start | bytes 12292
  702.3 297.9 %reduce-scatter.15.cloned.1.call-start = ((), (), s32[]{:S(2)}) async-start(), calls=%async_computation.16 | async-start | bytes 10485760 | tf_op jit(solution)/shard_map/reduce_scatter | solution.py:315
  713.2 434.4 %reduce-scatter.17.cloned.1.call-start = ((), (), s32[]{:S(2)}) async-start(), calls=%async_computation.17 | async-start | bytes 10485760 | tf_op jit(solution)/shard_map/reduce_scatter | solution.py:321
  723.9 532.5 %all-reduce.13.cloned.1.call-start = ((), (), s32[]{:S(2)}) async-start(), calls=%async_computation.18 | async-start | bytes 12582912 | tf_op jit(solution)/shard_map/psum | solution.py:331
  1164.8 41.2 %copy-start.3 = (f32[512,1024]{1,0:T(8,128)S(1)}, f32[512,1024]{1,0:T(8,128)}, u32[]{:S(2)}) copy-start(f32[512,1024]{1,0:T(8,128)} %copy-done.2) | copy-start | bytes 6291460
  1164.8 41.2 %copy-start.32 = (f32[512]{0:T(512)S(1)}, f32[512]{0:T(512)}, u32[]{:S(2)}) copy-start(f32[512]{0:T(512)} %copy-done.31) | copy-start | bytes 6148
  (40 other events, 321.6 us)
Sparse Core Ops, SparseCore 0:
  9.6 118.1 all-gather.13
  138.1 31.2 all-gather.15
  171.6 33.0 all-gather.17
  206.1 45.6 all-gather.19
  253.2 148.4 all-gather.21
  403.1 147.7 all-gather.23
  630.2 30.0 reduce-scatter.6
  662.5 31.8 reduce-scatter.8
  696.8 43.6 reduce-scatter.12
  742.6 109.9 reduce-scatter.10
  855.0 145.0 reduce-scatter.14
  1002.3 145.2 reduce-scatter.16
  1151.2 105.1 all-reduce.12
where the time goes:
time: 1280 us; the launch traced here: 1270 us
  waiting for transfers between devices  875 us (68%)
  matrix products  154 us (12%)
  blocking collectives  118 us (9%)
  local copies, waits for them, and re-layouts  64 us (5%)
  other arithmetic  43.8 us (3%)
  between operations  17.1 us (1%)
    reduce_scatter x1, waiting for transfers between devices, local(): lax.psum_scatter(terms[8].astype(jnp.bfloat16), 'fsdp', scatter_dimension...  147 us
    reduce_scatter x1, waiting for transfers between devices, local(): lax.psum_scatter(terms[10].astype(jnp.bfloat16), 'fsdp', scatter_dimensio...  147 us
    all_gather x1, waiting for transfers between devices, local(): lax.all_gather(shards[8], 'fsdp', axis=0, tiled=True)  146 us
    all_gather x1, waiting for transfers between devices, local(): lax.all_gather(shards[10], 'fsdp', axis=0, tiled=True)  122 us
    reduce_scatter x1, waiting for transfers between devices, local(): lax.psum_scatter(terms[2].astype(jnp.bfloat16), 'fsdp', scatter_dimension...  112 us
    all_gather x1, waiting for transfers between devices, local(): lax.all_gather(shards[2], 'fsdp', axis=0, tiled=True)  78.8 us
    psum x1, waiting for transfers between devices, local(): lax.psum(owned[2].astype(jnp.bfloat16), ('rep', 'seq')).astype(jnp.float32)  46.2 us
    reduce_scatter x1, waiting for transfers between devices, local(): lax.psum_scatter(value_grad.astype(jnp.bfloat16), 'seq', scatter_dimensio...  28.7 us
  transfers between devices with their start and end apart: 13, of which 12 were waited for; matrix products, arithmetic and copies ran while one was open for 12% of the time, Pallas kernels for 0%

commit v1 on v0

--- a/solution.py
+++ b/solution.py
@@ -4,6 +4,11 @@
 from jax.sharding import PartitionSpec as P
 
 epsilon = 1e-06
+
+
+def exchange_gather(x, name, along):
+    sent = jnp.stack([x] * lax.axis_size(name))
+    return jnp.concatenate(lax.all_to_all(sent, name, 0, 0), axis=along)
 
 
 def norm_rows(values, gains, shifts):
@@ -136,7 +141,7 @@
         lax.all_gather(shards[5], "fsdp", axis=0, tiled=True),
         lax.all_gather(shards[6], "fsdp", axis=0, tiled=True),
         lax.all_gather(shards[7], "fsdp", axis=0, tiled=True),
-        lax.all_gather(shards[8], "fsdp", axis=0, tiled=True),
+        exchange_gather(shards[8], "fsdp", 0),
         lax.all_gather(shards[9], "fsdp", axis=0, tiled=True),
         lax.all_gather(shards[10], "fsdp", axis=0, tiled=True),
         lax.all_gather(shards[11], "fsdp", axis=0, tiled=True),

time: 1280 us -> 1390 us (1.086)
  blocking collectives: 118 us -> 386 us
  waiting for transfers between devices: 875 us -> 700 us
    all_gather x1, blocking collectives: 7.97 us -> 174 us  [local(): lax.all_gather(shards[5], 'fsdp', axis=0, tiled=True)]
    all_gather x1, waiting for transfers between devices: 122 us -> 0.01 us  [local(): lax.all_gather(shards[10], 'fsdp', axis=0, tiled=True)]
    all_gather x1, blocking collectives: 11.9 us -> 111 us  [local(): lax.all_gather(shards[9], 'fsdp', axis=0, tiled=True)]
    all_gather x1, waiting for transfers between devices: 146 us -> 115 us  [local(): lax.all_gather(shards[8], 'fsdp', axis=0, tiled=True)]
    all_gather x1, waiting for transfers between devices: 15.6 us -> 0.02 us  [local(): lax.all_gather(shards[4], 'fsdp', axis=0, tiled=True)]
  transfers between devices with their start and end apart: 13 -> 14, of which waited for: 12 -> 9; matrix products, arithmetic and copies ran while one was open for 12% -> 13% of each run, Pallas kernels for 0% -> 0%
where the time goes in v1:
time: 1390 us; the launch traced here: 1380 us
  waiting for transfers between devices  700 us (50%)
  blocking collectives  386 us (28%)
  matrix products  156 us (11%)
  local copies, waits for them, and re-layouts  71.1 us (5%)
  other arithmetic  43.8 us (3%)
  between operations  17.1 us (1%)
    all_gather x1, blocking collectives, local(): lax.all_gather(shards[5], 'fsdp', axis=0, tiled=True)  174 us
    reduce_scatter x1, waiting for transfers between devices, local(): lax.psum_scatter(terms[8].astype(jnp.bfloat16), 'fsdp', scatter_dimension...  148 us
    reduce_scatter x1, waiting for transfers between devices, local(): lax.psum_scatter(terms[10].astype(jnp.bfloat16), 'fsdp', scatter_dimensio...  147 us
    all_gather x1, waiting for transfers between devices, local(): lax.all_gather(shards[8], 'fsdp', axis=0, tiled=True)  115 us
    reduce_scatter x1, waiting for transfers between devices, local(): lax.psum_scatter(terms[2].astype(jnp.bfloat16), 'fsdp', scatter_dimension...  112 us
    all_gather x1, blocking collectives, local(): lax.all_gather(shards[9], 'fsdp', axis=0, tiled=True)  111 us
    all_gather x1, waiting for transfers between devices, local(): lax.all_gather(shards[2], 'fsdp', axis=0, tiled=True)  78.8 us
    psum x1, waiting for transfers between devices, local(): lax.psum(owned[2].astype(jnp.bfloat16), ('rep', 'seq')).astype(jnp.float32)  46.2 us
  transfers between devices with their start and end apart: 14, of which 9 were waited for; matrix products, arithmetic and copies ran while one was open for 13% of the time, Pallas kernels for 0%

profile of v1, /device:TPU:0, one launch (start us, length us, event | category | flops | bytes accessed | tf_op | source)
XLA Modules:
  0.0 1381.7 jit_solution(17116113935965499209)
XLA Ops:
  8.6 14.8 %all-gather.2 = bf16[4,1,768]{2,1,0:T(2,128)(2,1)S(1)} all-gather(bf16[1,1,768]{2,1,0:T(2,128)(2,1)S(1)} %reshape.250), channel_id=1, replica_groups=mesh['rep'=4,'fsdp'=4,'seq'=2] {'fsdp'}, dimensions={0}, use_global_device_ids=true | all-gather | bytes 7680 | tf_op jit(solution)/shard_map/all_gather | solution.py:139
  24.2 12.4 all-gather.1
  37.3 8.0 all-gather
  49.0 78.8 %all-gather.14.cloned.1.call-done = bf16[1024,3072]{1,0:T(8,128)(2,1)} async-done(((bf16[256,3072]{1,0:T(8,128)(2,1)}), bf16[1024,3072]{1,0:T(8,128)(2,1)}) %all-gather.14.cloned.1.call-update) | async-done | bytes 6291472 | tf_op jit(solution)/shard_map/all_gather | solution.py:138
  127.8 6.1 convolution_add_fusion
  139.2 4.9 fusion.45
  158.6 5.9 stack.16
  164.5 5.8 all-to-all-start
  171.1 174.3 %all-gather.3 = bf16[4,1,256]{2,1,0:T(2,128)(2,1)S(1)} all-gather(bf16[1,1,256]{2,1,0:T(2,128)(2,1)S(1)} %reshape.252), channel_id=1, replica_groups=mesh['rep'=4,'fsdp'=4,'seq'=2] {'fsdp'}, dimensions={0}, use_global_device_ids=true | all-gather | bytes 2560 | tf_op jit(solution)/shard_map/all_gather | solution.py:141
  345.4 111.5 %all_gather.57 = bf16[4096]{0:T(1024)(128)(2,1)S(1)} all-gather(bf16[1024]{0:T(1024)(128)(2,1)S(1)} %copy-done.50), channel_id=1, replica_groups=mesh['rep'=4,'fsdp'=4,'seq'=2] {'fsdp'}, dimensions={0}, use_global_device_ids=true | all-gather | bytes 10240 | tf_op jit(solution)/shard_map/all_gather | solution.py:145
  456.9 9.4 all-gather.5
  466.3 10.6 all-gather.4
  479.0 31.4 %while.30 = (s32[]{:T(128)}, bf16[4,512,256]{1,2,0:T(8,128)(2,1)S(1)}, f32[4,4,512,1]{2,1,3,0:T(4,128)S(1)}, f32[4,4,512,1]{2,1,3,0:T(4,128)S(1)}, bf16[4,1024,2...) while((s32[]{:T(128)}, ...), condition=%wide.region_5.6_spmd.clone, body=%wide.region_2.5_spmd.sunk.clone | while | flops 555741184 | bytes 29958248 | solution.py:190
  515.4 27.9 %multiply_convert_fusion.1 = (bf16[512,4096]{1,0:T(8,128)(2,1)}, f32[512,4096]{1,0:T(8,128)}, f32[512,4096]{1,0:T(8,128)}) fusion(f32[4096]{0:T(1024)S(1)} %convert_element_type.220, bf16[1024,4096]{1,0:T(8,128)(2,1)} %bitcast.41, f32[512,1024]{1,0:T(8,128)S(1)} %get-tuple-element.210, f32[1024]{0:T(1024)S(1)} %bitcast.296, f32[1024]{0:T(1024)S(1)} %bitcast.289, ...), kind=kOutput, calls=%fused_computation.31 | convolution fusion | flops 4436000768 | bytes 31485952 | tf_op jit(solution)/shard_map/dot_general | solution.py:199
  543.3 15.8 %fusion.47 = (bf16[4096]{0:T(1024)(128)(2,1)}, bf16[512,4096]{1,0:T(8,128)(2,1)}) fusion(f32[512,4096]{1,0:T(8,128)} %get-tuple-element.179, bf16[4096,1024]{1,0:T(8,128)(2,1)} %all-gather.22.cloned.1.call-done, bf16[1,512,1024]{2,1,0:T(8,128)(2,1)S(1)} %copy-done.7, f32[512,4096]{1,0:T(8,128)} %get-tuple-element.211, f32[4096]{0:T(1024)S(1)} %convert_element_type.220), kind=kOutput, calls=%fused_computation.125 | convolution fusion | flops 4328517632 | bytes 30433280 | tf_op jit(solution)/shard_map/td,fd->tf/dot_general | solution.py:226
  559.1 114.5 %all-gather.24.cloned.1.call-done = bf16[1024,4096]{1,0:T(8,128)(2,1)} async-done(((bf16[256,4096]{1,0:T(8,128)(2,1)}), bf16[1024,4096]{1,0:T(8,128)(2,1)}) %all-gather.24.cloned.1.call-update) | async-done | bytes 8388624 | tf_op jit(solution)/shard_map/all_gather | solution.py:217
  673.6 9.3 multiply_reduce_fusion.2
  690.8 47.8 %while.31 = (s32[]{:T(128)}, f32[4,512,256]{1,2,0:T(8,128)S(1)}, bf16[4,1024,256]{1,2,0:T(8,128)(2,1)}, bf16[4,1024,256]{1,2,0:T(8,128)(2,1)}, bf16[4,1024,256]{...) while((s32[]{:T(128)}, f32[4,512,256]{1,2,0:T(8,128)S(1)}, ...), condition=%wide.region_12.13_spmd.clone, body=%wide.region_10.12_spmd.sunk.clone | while | flops 1361704960 | bytes 73465992 | solution.py:247
  747.6 21.4 %reduce-scatter.7.cloned.1.call-done = bf16[4,512,256]{1,2,0:T(8,128)(2,1)} async-done(((bf16[4,1024,256]{1,2,0:T(8,128)(2,1)}), bf16[4,512,256]{1,2,0:T(8,128)(2,1)}) %reduce-scatter.7.cloned.1.call-update) | async-done | bytes 1048592 | tf_op jit(solution)/shard_map/reduce_scatter | solution.py:252
  774.4 28.7 %reduce-scatter.9.cloned.1.call-done = bf16[4,512,256]{1,2,0:T(8,128)(2,1)} async-done(((bf16[4,1024,256]{1,2,0:T(8,128)(2,1)}), bf16[4,512,256]{1,2,0:T(8,128)(2,1)}) %reduce-scatter.9.cloned.1.call-update) | async-done | bytes 1048592 | tf_op jit(solution)/shard_map/reduce_scatter | solution.py:255
  803.2 7.8 convolution_convert_fusion.2
  812.7 9.2 convolution_convert_fusion.1
  822.2 10.4 convolution_convert_fusion
  833.2 11.5 all-gather.6
  849.1 112.2 %reduce-scatter.11.cloned.1.call-done = bf16[256,3072]{1,0:T(8,128)(2,1)} async-done(((bf16[1024,3072]{1,0:T(8,128)(2,1)}), bf16[256,3072]{1,0:T(8,128)(2,1)}) %reduce-scatter.11.cloned.1.call-update) | async-done | bytes 1572880 | tf_op jit(solution)/shard_map/reduce_scatter | solution.py:302
  961.3 147.5 %reduce-scatter.15.cloned.1.call-done = bf16[256,4096]{1,0:T(8,128)(2,1)} async-done(((bf16[1024,4096]{1,0:T(8,128)(2,1)}), bf16[256,4096]{1,0:T(8,128)(2,1)}) %reduce-scatter.15.cloned.1.call-update) | async-done | bytes 2097168 | tf_op jit(solution)/shard_map/reduce_scatter | solution.py:320
  1108.8 147.5 %reduce-scatter.17.cloned.1.call-done = bf16[1024,1024]{1,0:T(8,128)(2,1)} async-done(((bf16[4096,1024]{1,0:T(8,128)(2,1)}), bf16[1024,1024]{1,0:T(8,128)(2,1)}) %reduce-scatter.17.cloned.1.call-update) | async-done | bytes 2097168 | tf_op jit(solution)/shard_map/reduce_scatter | solution.py:326
  1256.4 10.3 fusion.24
  1266.6 6.8 fusion.40
  1275.8 18.9 %all-reduce.10 = (bf16[1024]{0:T(1024)(128)(2,1)S(1)}, bf16[1024]{0:T(1024)(128)(2,1)S(1)}, bf16[3072]{0:T(1024)(128)(2,1)S(1)}, bf16[1024]{0:T(1024)(128)(2,1)S...) all-reduce(bf16[1024]{0:T(1024)(128)(2,1)S(1)} %get-tuple-element.1, ...), channel_id=4, replica_groups=mesh['rep'=4,'fsdp'=4,'seq'=2] {'fsdp'}, use_global_device_ids=true, to_apply=%region_18.19.clone | all-reduce | flops 13312 | bytes 53248
  1295.3 14.9 %all-reduce.8 = (bf16[256]{0:T(256)(128)(2,1)S(1)}, bf16[256]{0:T(256)(128)(2,1)S(1)}, bf16[768]{0:T(1024)(128)(2,1)S(1)}, bf16[256]{0:T(256)(128)(2,1)S(1)}, bf...) all-reduce(bf16[256]{0:T(256)(128)(2,1)S(1)} %dynamic-slice.1, ...), channel_id=1, replica_groups=mesh['rep'=4,'fsdp'=4,'seq'=2] {'rep','seq'}, use_global_device_ids=true, to_apply=%region_19.20 | all-reduce | flops 3328 | bytes 13312 | tf_op jit(solution)/shard_map/psum | solution.py:334
  1318.9 46.2 %all-reduce.13.cloned.1.call-done = (bf16[256,3072]{1,0:T(8,128)(2,1)}, bf16[256,1024]{1,0:T(8,128)(2,1)}, bf16[256,4096]{1,0:T(8,128)(2,1)}, bf16[1024,1024]{1,0:T(8,128)(2,1)}) async-done(((bf16[256,3072]{1,0:T(8,128)(2,1)}, bf16[256,1024]{1,0:T(8,128)(2,1)}, bf16[256,4096]{1,0:T(8,128)(2,1)}, bf16[1024,1024]{1,0:T(8,128)(2,1)}), (bf16[256,3072]{1,0:T(8,128)(2,1)}, bf16[256,1024]{1,0:T(8,128)(2,1)}, ...) | async-done | bytes 6291472 | tf_op jit(solution)/shard_map/psum | solution.py:336
  (325 shorter events, 161.1 us)
Async XLA Ops:
  7.2 120.6 %all-gather.14.cloned.1.call-start = ((), (), s32[]{:S(2)}) async-start(), calls=%async_computation.7 | async-start | bytes 7864320 | tf_op jit(solution)/shard_map/all_gather | solution.py:138
  7.9 471.0 %all-gather.16.cloned.1.call-start = ((), (), s32[]{:S(2)}) async-start(), calls=%async_computation.8 | async-start | bytes 3145728 | tf_op jit(solution)/shard_map/all_gather | solution.py:188
  36.6 91.2 %copy-start.46 = (f32[4,1,256]{2,1,0:T(1,128)}, f32[4,1,256]{2,1,0:T(1,128)S(1)}, u32[]{:S(2)}) copy-start(f32[4,1,256]{2,1,0:T(1,128)S(1)} %convert_element_type.251) | copy-start | bytes 12292
  45.3 82.5 %copy-start.27 = (f32[4,1,256]{2,1,0:T(1,128)}, f32[4,1,256]{2,1,0:T(1,128)S(1)}, u32[]{:S(2)}) copy-start(f32[4,1,256]{2,1,0:T(1,128)S(1)} %convert_element_type.250) | copy-start | bytes 12292
  46.7 81.0 %copy-start.29 = (f32[512]{0:T(512)}, f32[512]{0:T(512)S(1)}, u32[]{:S(2)}) copy-start(f32[512]{0:T(512)S(1)} %broadcast_multiply_fusion.1) | copy-start | bytes 6148
  49.0 78.8 %copy-start.35 = (f32[512]{0:T(512)}, f32[512]{0:T(512)S(1)}, u32[]{:S(2)}) copy-start(f32[512]{0:T(512)S(1)} %fusion.32) | copy-start | bytes 6148
  138.0 340.9 %all-gather.18.cloned.1.call-start = ((), (), s32[]{:S(2)}) async-start(), calls=%async_computation.9 | async-start | bytes 3145728 | tf_op jit(solution)/shard_map/all_gather | solution.py:187
  157.5 353.0 %all-gather.20.cloned.1.call-start = ((), (), s32[]{:S(2)}) async-start(), calls=%async_computation.10 | async-start | bytes 2621440 | tf_op jit(solution)/shard_map/all_gather | solution.py:140
  158.0 385.3 %all-gather.22.cloned.1.call-start = ((), (), s32[]{:S(2)}) async-start(), calls=%async_computation.11 | async-start | bytes 10485760 | tf_op jit(solution)/shard_map/all_gather | solution.py:146
  164.5 180.9 %copy-start.50 = (bf16[1024]{0:T(1024)(128)(2,1)S(1)}, bf16[1024]{0:T(1024)(128)(2,1)}, u32[]{:S(2)}) copy-start(bf16[1024]{0:T(1024)(128)(2,1)} %param.30) | copy-start | bytes 6148
  164.5 292.3 %copy-start.54 = (bf16[256]{0:T(256)(128)(2,1)S(1)}, bf16[256]{0:T(256)(128)(2,1)}, u32[]{:S(2)}) copy-start(bf16[256]{0:T(256)(128)(2,1)} %param.28) | copy-start | bytes 1540
  164.5 301.8 %copy-start.55 = (bf16[256]{0:T(256)(128)(2,1)S(1)}, bf16[256]{0:T(256)(128)(2,1)}, u32[]{:S(2)}) copy-start(bf16[256]{0:T(256)(128)(2,1)} %param.27) | copy-start | bytes 1540
  164.5 350.9 %all-to-all-start = ((bf16[4,256,4096]{2,1,0:T(8,128)(2,1)}), bf16[4,256,4096]{2,1,0:T(8,128)(2,1)}, u32[]{:S(2)}, u32[]{:S(2)}) async-start(bf16[4,256,4096]{2,1,0:T(8,128)(2,1)} %stack.16), calls=%async_computation | async-start | bytes 16777216 | tf_op jit(solution)/shard_map/all_to_all | solution.py:11
  170.3 503.3 %all-gather.24.cloned.1.call-start = ((), (), s32[]{:S(2)}) async-start(), calls=%async_computation.12 | async-start | bytes 10485760 | tf_op jit(solution)/shard_map/all_gather | solution.py:217
  170.9 598.0 %reduce-scatter.7.cloned.1.call-start = ((), (), s32[]{:S(2)}) async-start(), calls=%async_computation.13 | async-start | bytes 3145728 | tf_op jit(solution)/shard_map/reduce_scatter | solution.py:252
  466.3 49.1 %copy-start.48 = (f32[4,1,256]{2,1,0:T(1,128)}, f32[4,1,256]{2,1,0:T(1,128)S(1)}, u32[]{:S(2)}) copy-start(f32[4,1,256]{2,1,0:T(1,128)S(1)} %convert_element_type.255) | copy-start | bytes 12292
  477.0 206.0 %copy-start.39 = (f32[4,1,256]{2,1,0:T(1,128)}, f32[4,1,256]{2,1,0:T(1,128)S(1)}, u32[]{:S(2)}) copy-start(f32[4,1,256]{2,1,0:T(1,128)S(1)} %convert_element_type.254) | copy-start | bytes 12292
  479.0 32.8 %copy-start = (bf16[1,512,1024]{2,1,0:T(8,128)(2,1)S(1)}, bf16[1,512,1024]{2,1,0:T(8,128)(2,1)}, u32[]{:S(2)}) copy-start(bf16[1,512,1024]{2,1,0:T(8,128)(2,1)} %param.19) | copy-start | bytes 3145732
  515.0 167.9 %copy-start.4 = (f32[512,1024]{1,0:T(8,128)}, f32[512,1024]{1,0:T(8,128)S(1)}, u32[]{:S(2)}) copy-start(f32[512,1024]{1,0:T(8,128)S(1)} %get-tuple-element.210) | copy-start | bytes 6291460
  515.0 167.9 %copy-start.37 = (f32[512]{0:T(512)}, f32[512]{0:T(512)S(1)}, u32[]{:S(2)}) copy-start(f32[512]{0:T(512)S(1)} %broadcast_multiply_fusion) | copy-start | bytes 6148
  515.4 167.6 %copy-start.42 = (f32[512]{0:T(512)}, f32[512]{0:T(512)S(1)}, u32[]{:S(2)}) copy-start(f32[512]{0:T(512)S(1)} %fusion.33) | copy-start | bytes 6148
  738.7 64.4 %reduce-scatter.9.cloned.1.call-start = ((), (), s32[]{:S(2)}) async-start(), calls=%async_computation.14 | async-start | bytes 3145728 | tf_op jit(solution)/shard_map/reduce_scatter | solution.py:255
  739.4 109.7 %reduce-scatter.13.cloned.1.call-start = ((), (), s32[]{:S(2)}) async-start(), calls=%async_computation.16 | async-start | bytes 2621440 | tf_op jit(solution)/shard_map/reduce_scatter | solution.py:308
  744.5 216.8 %reduce-scatter.11.cloned.1.call-start = ((), (), s32[]{:S(2)}) async-start(), calls=%async_computation.15 | async-start | bytes 7864320 | tf_op jit(solution)/shard_map/reduce_scatter | solution.py:302
  773.0 30.2 %copy-start.1 = (bf16[1,512,1024]{2,1,0:T(8,128)(2,1)S(1)}, bf16[1,512,1024]{2,1,0:T(8,128)(2,1)}, u32[]{:S(2)}) copy-start(bf16[1,512,1024]{2,1,0:T(8,128)(2,1)} %param.19) | copy-start | bytes 3145732
  773.0 30.1 %copy-start.28 = (f32[4,1,256]{2,1,0:T(1,128)S(1)}, f32[4,1,256]{2,1,0:T(1,128)}, u32[]{:S(2)}) copy-start(f32[4,1,256]{2,1,0:T(1,128)} %copy-done.27) | copy-start | bytes 12292
  773.0 30.1 %copy-start.30 = (f32[512]{0:T(512)S(1)}, f32[512]{0:T(512)}, u32[]{:S(2)}) copy-start(f32[512]{0:T(512)} %copy-done.29) | copy-start | bytes 6148
  811.0 297.9 %reduce-scatter.15.cloned.1.call-start = ((), (), s32[]{:S(2)}) async-start(), calls=%async_computation.17 | async-start | bytes 10485760 | tf_op jit(solution)/shard_map/reduce_scatter | solution.py:320
  821.9 434.4 %reduce-scatter.17.cloned.1.call-start = ((), (), s32[]{:S(2)}) async-start(), calls=%async_computation.18 | async-start | bytes 10485760 | tf_op jit(solution)/shard_map/reduce_scatter | solution.py:326
  832.6 532.5 %all-reduce.13.cloned.1.call-start = ((), (), s32[]{:S(2)}) async-start(), calls=%async_computation.19 | async-start | bytes 12582912 | tf_op jit(solution)/shard_map/psum | solution.py:336
  1273.5 41.2 %copy-start.3 = (f32[512,1024]{1,0:T(8,128)S(1)}, f32[512,1024]{1,0:T(8,128)}, u32[]{:S(2)}) copy-start(f32[512,1024]{1,0:T(8,128)} %copy-done.2) | copy-start | bytes 6291460
  1273.5 41.2 %copy-start.32 = (f32[512]{0:T(512)S(1)}, f32[512]{0:T(512)}, u32[]{:S(2)}) copy-start(f32[512]{0:T(512)} %copy-done.31) | copy-start | bytes 6148
  (40 other events, 332.9 us)
Sparse Core Ops, SparseCore 0:
  9.6 118.1 all-gather.13
  138.1 31.2 all-gather.15
  171.6 33.0 all-gather.17
  206.1 75.7 all-gather.19
  283.4 240.1 all-gather.21
  525.0 148.6 all-gather.23
  738.8 30.0 reduce-scatter.6
  771.2 31.8 reduce-scatter.8
  805.4 43.6 reduce-scatter.12
  851.3 109.9 reduce-scatter.10
  963.7 145.1 reduce-scatter.14
  1111.0 145.2 reduce-scatter.16
  1259.9 105.1 all-reduce.12
